TPU v7x, 128 devices: a whole 4x4x4 slice. The times are simulated.
128 devices in a mesh: feat: 32 (over z, x_hi, y), ex: 4 (over x_lo, core).
Axes of the slice: x: 4 (x_hi: 2, x_lo: 2; x = x_hi * 2 + x_lo), y: 4, z: 4, core: 2. Of those that a mesh axis runs over, the one named last changes fastest.
Arguments:
- grads: bfloat16 [256, 4194304], P('ex', 'feat'), may hold values from -6 to 6
- sign_bits: int32 [4194304], P('feat'), may hold values from 0 to 1
- sample_offset: int32 [8192], replicated, may hold values from 0 to 511
- queries: bfloat16 [16384, 8192], P('ex', 'feat'), may hold values from -6 to 6
- panel_order: int32 [32], replicated, may hold values from 0 to 31, each once
Outputs:
- scores: float32 [256, 16384], P('ex', 'feat')
Inputs may be any that keep to these rules, and one draw needn't show every extreme that they name: sample_offset is below 512. panel_order is a permutation.
All inputs are finite; a program needn't handle non-finite values.
Results may differ from a plain program's by a relative error of at most 0.018.
Values may be sent and summed in bfloat16 or wider, within the bound.
No kernel may reach another device: no remote copies, remote signals or barrier semaphores. Data moves between devices by JAX's collectives and lax.ppermute only.
A program may use at most 192 MiB of HBM per device.

v0:
```python
import math
import jax
import jax.numpy as jnp
from jax import lax
from jax.sharding import PartitionSpec as P

HA = 256
HB = 512
PROJ = 8192


def parity_of(values, bits):
    total = jnp.zeros_like(values)
    for position in range(bits):
        total = total ^ values >> position & 1
    return total


def hadamard_table(order, scale, dtype):
    index = jnp.arange(order, dtype=jnp.int32)
    parity = parity_of(index[:, None] & index[None, :], order.bit_length() - 1)
    return ((1 - 2 * parity).astype(jnp.float32) * scale).astype(dtype)


def hadamard_rows(index, order, scale):
    column = jnp.arange(order, dtype=jnp.int32)
    parity = parity_fold(index[..., None] & column, order.bit_length() - 1)
    return ((1 - 2 * parity).astype(jnp.float32) * scale).astype(jnp.bfloat16)


def parity_fold(values, bits):
    shift = 1
    while shift < bits:
        shift *= 2
    while shift >= 1:
        values = values ^ values >> shift
        shift //= 2
    return values & 1


def power_scale(order):
    return 0.5 ** ((order.bit_length() - 1) // 2)


def on_device(grads, sign_bits, sample_offset, queries, panel_order):
    shards = lax.axis_size("feat")
    examples, feat_dev = grads.shape
    proj_dev = PROJ // shards
    scale_b = power_scale(HB)
    scale_a = power_scale(HA)
    cross = power_scale(feat_dev * shards) / (scale_a * scale_b)
    device_id = lax.axis_index("feat")
    signed = grads * (1 - 2 * sign_bits).astype(jnp.bfloat16)[None, :]
    table_a = hadamard_table(HA, scale_a, jnp.bfloat16)
    turned = jnp.einsum(
        "ca,eab->ceb", table_a, signed.reshape(examples, HA, HB), preferred_element_type=jnp.float32
    )
    rows = hadamard_rows(sample_offset.reshape(shards, proj_dev), HB, scale_b)
    picked = lax.dot_general(
        turned.astype(jnp.bfloat16),
        rows,
        (((2,), (2,)), ((0,), (1,))),
        preferred_element_type=jnp.float32,
    )
    local = picked.astype(jnp.bfloat16)
    full_table = hadamard_table(shards, 1.0, jnp.bfloat16)
    signs = lax.dynamic_slice_in_dim(full_table, device_id, 1, 1)[:, 0]
    outgoing = jnp.transpose(local, (2, 1, 0)) * signs[:, None, None]
    returned = lax.all_to_all(outgoing, "feat", split_axis=0, concat_axis=0, tiled=True)
    projected = (jnp.sum(returned.astype(jnp.float32), axis=0) * cross).astype(jnp.bfloat16)
    every = lax.all_gather(projected, "ex", axis=0, tiled=True)
    ex_count = lax.axis_size("ex")
    panel_count = panel_order.shape[0]
    per_row = panel_count // ex_count
    partial_value = lax.dot_general(
        every.reshape(ex_count, examples, -1),
        queries.reshape(per_row, -1, queries.shape[1]),
        (((2,), (2,)), ((), ())),
        preferred_element_type=jnp.float32,
    )
    partial_value = jnp.transpose(partial_value * (1.0 / math.sqrt(PROJ)), (0, 2, 1, 3))
    partial_value = partial_value.astype(jnp.bfloat16)
    mine = lax.all_to_all(partial_value, "ex", split_axis=0, concat_axis=0, tiled=True)
    ordered = jnp.take(mine.reshape(panel_count, examples, -1), panel_order, axis=0, mode="clip")
    gathered = lax.all_to_all(ordered, "feat", split_axis=0, concat_axis=0, tiled=True)
    return jnp.sum(gathered.astype(jnp.float32), axis=0)


def solution(mesh):
    in_specs = (P("ex", "feat"), P("feat"), P(), P("ex", "feat"), P())
    out_specs = P("ex", "feat")
    return jax.shard_map(
        on_device, mesh=mesh, in_specs=in_specs, out_specs=out_specs, check_vma=False
    )
```

profile of v0, /device:TPU:8, one launch (start us, length us, event | category | flops | bytes accessed | tf_op | source)
XLA Modules:
  0.0 161.5 jit_solution(10771877939283327149)
XLA Ops:
  0.0 0.0 copy-start
  0.0 1.2 subtract_convert_fusion
  1.3 8.5 %broadcast_multiply_fusion = bf16[64,131072]{1,0:T(8,128)(2,1)S(1)} fusion(bf16[64,131072]{1,0:T(8,128)(2,1)} %param.5, bf16[131072]{0:T(1024)(128)(2,1)S(1)} %subtract_convert_fusion), kind=kLoop, calls=%fused_computation.22 | loop fusion | flops 8388608 | bytes 33816576 | tf_op jit(solution)/shard_map/mul | solution.py:53
  9.8 8.8 %copy.24 = bf16[8,8,256,512]{3,2,1,0:T(8,128)(2,1)} copy(bf16[8,8,256,512]{3,1,2,0:T(8,128)(2,1)S(1)} %bitcast.25) | data formatting | bytes 33554432
  18.6 0.0 copy-start.1
  18.6 14.0 %convolution_convert_fusion = bf16[256,64,512]{2,0,1:T(8,128)(2,1)} fusion(bf16[64,256,512]{2,1,0:T(8,128)(2,1)} %bitcast.24), kind=kOutput, calls=%fused_computation.14 | convolution fusion | flops 4305256448 | bytes 33554432 | tf_op jit(solution)/shard_map/ca,eab->ceb/dot_general | solution.py:55
  32.5 0.0 copy-done.1
  32.6 0.1 copy.17
  32.7 0.0 copy-start.2
  32.7 20.6 %multiply_bitcast_fusion = bf16[32,64,256]{1,0,2:T(8,128)(2,1)} fusion(s32[32,256]{0,1:T(8,128)S(1)} %copy.17, bf16[256,64,512]{2,0,1:T(8,128)(2,1)} %convolution_convert_fusion, bf16[32]{0:T(256)(128)(2,1)S(1)} %convert_bitcast_fusion), kind=kOutput, calls=%fused_computation.26 | convolution fusion | flops 609222656 | bytes 17858624 | tf_op jit(solution)/shard_map/dot_general | solution.py:59
  53.3 2.8 %copy.19 = bf16[32,64,256]{2,1,0:T(8,128)(2,1)S(1)} copy(bf16[32,64,256]{1,0,2:T(8,128)(2,1)} %multiply_bitcast_fusion) | data formatting | bytes 2097152 | tf_op jit(solution)/shard_map/mul | solution.py:68
  56.1 28.7 %all_to_all.15 = bf16[32,64,256]{2,1,0:T(8,128)(2,1)S(1)} all-to-all(bf16[32,64,256]{2,1,0:T(8,128)(2,1)S(1)} %copy.19), channel_id=1, replica_groups=mesh['feat'=32,'ex'=4] {'feat'}, dimensions={0} | all-to-all | bytes 2097152 | tf_op jit(solution)/shard_map/all_to_all | solution.py:69
  84.8 0.2 convert_reduce_fusion.1
  84.9 5.4 %all_gather.3 = bf16[256,256]{1,0:T(8,128)(2,1)S(1)} all-gather(bf16[64,256]{1,0:T(8,128)(2,1)S(1)} %multiply_convert_fusion.2), channel_id=1, replica_groups=mesh['feat'=32,'ex'=4] {'ex'}, dimensions={0}, use_global_device_ids=true | all-gather | bytes 163840 | tf_op jit(solution)/shard_map/all_gather | solution.py:71
  90.4 0.0 copy-done
  90.4 2.1 %fusion.20 = bf16[4,8,64,512]{3,2,1,0:T(8,128)(2,1)} fusion(bf16[4,64,256,1]{2,1,3,0:T(8,128)(2,1)S(1)} %bitcast.26, bf16[8,512,256,1]{2,1,0,3:T(8,128)(2,1)S(1)} %bitcast.23), kind=kOutput, calls=%fused_computation.27 | convolution fusion | flops 538968064 | bytes 4325376 | tf_op jit(solution)/shard_map/dot_general | solution.py:75
  92.4 4.4 %all-to-all-start.1 = ((bf16[4,8,64,512]{3,2,1,0:T(8,128)(2,1)}), bf16[4,8,64,512]{3,2,1,0:T(8,128)(2,1)}, u32[]{:S(2)}, u32[]{:S(2)}) async-start(bf16[4,8,64,512]{3,2,1,0:T(8,128)(2,1)} %fusion.20), calls=%async_computation.1 | async-start | bytes 4194304 | tf_op jit(solution)/shard_map/all_to_all | solution.py:83
  96.8 0.0 copy-done.2
  96.9 25.7 %all-to-all-done.1 = bf16[4,8,64,512]{3,2,1,0:T(8,128)(2,1)} async-done(((bf16[4,8,64,512]{3,2,1,0:T(8,128)(2,1)}), bf16[4,8,64,512]{3,2,1,0:T(8,128)(2,1)}, u32[]{:S(2)}, u32[]{:S(2)}) %all-to-all-start.1) | async-done | bytes 2097184 | tf_op jit(solution)/shard_map/all_to_all | solution.py:83
  122.6 3.6 %gather_fusion = bf16[32,64,512]{2,1,0:T(8,128)(2,1)} fusion(bf16[32,64,512]{2,1,0:T(8,128)(2,1)} %bitcast.9, s32[1024]{0:T(1024)S(1)} %pad_clamp_fusion), kind=kCustom, calls=%fused_computation | custom fusion | bytes 4194432 | tf_op jit(solution)/shard_map/jit(_take)/gather | solution.py:84
  126.2 34.4 %all_to_all.16 = bf16[32,64,512]{2,1,0:T(8,128)(2,1)S(1)} all-to-all(bf16[32,64,512]{2,1,0:T(8,128)(2,1)} %gather_fusion), channel_id=1, replica_groups=mesh['feat'=32,'ex'=4] {'feat'}, dimensions={0} | all-to-all | bytes 4194304 | tf_op jit(solution)/shard_map/all_to_all | solution.py:85
  160.5 0.9 convert_reduce_fusion
  (6 shorter events, 0.1 us)
Async XLA Ops:
  0.0 90.4 %copy-start = (bf16[4096,256]{1,0:T(8,128)(2,1)S(1)}, bf16[4096,256]{1,0:T(8,128)(2,1)}, u32[]{:S(2)}) copy-start(bf16[4096,256]{1,0:T(8,128)(2,1)} %param.8) | copy-start | bytes 6291460
  18.6 14.0 %copy-start.1 = (s32[8192]{0:T(1024)S(1)}, s32[8192]{0:T(1024)}, u32[]{:S(2)}) copy-start(s32[8192]{0:T(1024)} %param.7) | copy-start | bytes 98308
  32.7 64.2 %copy-start.2 = (s32[32]{0:T(128)S(1)}, s32[32]{0:T(128)}, u32[]{:S(2)}) copy-start(s32[32]{0:T(128)} %param.9) | copy-start | bytes 388
  92.4 30.2 %all-to-all-start.1 = ((bf16[4,8,64,512]{3,2,1,0:T(8,128)(2,1)}), bf16[4,8,64,512]{3,2,1,0:T(8,128)(2,1)}, u32[]{:S(2)}, u32[]{:S(2)}) async-start(bf16[4,8,64,512]{3,2,1,0:T(8,128)(2,1)} %fusion.20), calls=%async_computation.1 | async-start | bytes 4194304 | tf_op jit(solution)/shard_map/all_to_all | solution.py:83
where the time goes:
time: 162 us; the launch traced here: 161 us
  blocking collectives  68.5 us (42%)
  matrix products  36.6 us (23%)
  waiting for transfers between devices  25.7 us (16%)
  local copies, waits for them, and re-layouts  15.3 us (9%)
  other arithmetic  10.9 us (7%)
  starting transfers between devices  4.43 us (3%)
    all_to_all x1, blocking collectives, on_device(): lax.all_to_all(ordered, 'feat', split_axis=0, concat_axis=0, tiled=True)  34.4 us
    all_to_all x1, blocking collectives, on_device(): lax.all_to_all(outgoing, 'feat', split_axis=0, concat_axis=0, tiled=True)  28.7 us
    all_to_all x1, waiting for transfers between devices, on_device(): lax.all_to_all(partial_value, 'ex', split_axis=0, concat_axis=0, tiled=True)  25.7 us
    dot_general x1, matrix products, on_device(): lax.dot_general(turned.astype(jnp.bfloat16), rows, (((2,), (2,)), ((0,),...  20.6 us
    dot_general x1, matrix products, on_device(): jnp.einsum('ca,eab->ceb', table_a, signed.reshape(examples, HA, HB), pref...  14 us
    unnamed x7, local copies, waits for them, and re-layouts  8.79 us
    mul x1, other arithmetic, on_device(): signed = grads * (1 - 2 * sign_bits).astype(jnp.bfloat16)[None, :]  8.52 us
    all_gather x1, blocking collectives, on_device(): every = lax.all_gather(projected, 'ex', axis=0, tiled=True)  5.42 us
  transfers between devices with their start and end apart: 1, of which 1 were waited for; matrix products, arithmetic and copies ran while one was open for 0% of the time, Pallas kernels for 0%

commit v1 on v0

--- a/solution.py
+++ b/solution.py
@@ -68,7 +68,9 @@
     outgoing = jnp.transpose(local, (2, 1, 0)) * signs[:, None, None]
     returned = lax.all_to_all(outgoing, "feat", split_axis=0, concat_axis=0, tiled=True)
     projected = (jnp.sum(returned.astype(jnp.float32), axis=0) * cross).astype(jnp.bfloat16)
-    every = lax.all_gather(projected, "ex", axis=0, tiled=True)
+    every = jnp.concatenate(
+        lax.all_to_all(jnp.stack([projected] * lax.axis_size("ex")), "ex", 0, 0), axis=0
+    )
     ex_count = lax.axis_size("ex")
     panel_count = panel_order.shape[0]
     per_row = panel_count // ex_count

time: 162 us -> 180 us (1.11)
  other arithmetic: 10.9 us -> 21.6 us
  matrix products: 36.6 us -> 42.1 us
    convert_element_type x0 -> x1, other arithmetic: none -> 10.6 us  [hadamard_rows(): return ((1 - 2 * parity).astype(jnp.float32) * scale).astype(jnp.bfloat16)]
    all_to_all x0 -> x1, blocking collectives: none -> 6.99 us  [on_device(): lax.all_to_all(jnp.stack([projected] * lax.axis_size('ex')), 'ex', 0, 0)]
    dot_general x1, matrix products: 20.6 us -> 26.1 us  [on_device(): lax.dot_general(turned.astype(jnp.bfloat16), rows, (((2,), (2,)), ((0,),...]
    all_gather x1 -> x0, blocking collectives: 5.42 us -> none  [on_device(): every = lax.all_gather(projected, 'ex', axis=0, tiled=True)]
    dot_general x0 -> x1, local copies, waits for them, and re-layouts: none -> 2.8 us  [on_device(): lax.dot_general(turned.astype(jnp.bfloat16), rows, (((2,), (2,)), ((0,),...]
    mul x1 -> x0, local copies, waits for them, and re-layouts: 2.79 us -> none  [on_device(): outgoing = jnp.transpose(local, (2, 1, 0)) * signs[:, None, None]]
where the time goes in v1:
time: 180 us; the launch traced here: 179 us
  blocking collectives  70 us (39%)
  matrix products  42.1 us (23%)
  waiting for transfers between devices  25.7 us (14%)
  other arithmetic  21.6 us (12%)
  local copies, waits for them, and re-layouts  15.2 us (8%)
  starting transfers between devices  4.43 us (2%)
    all_to_all x1, blocking collectives, on_device(): lax.all_to_all(ordered, 'feat', split_axis=0, concat_axis=0, tiled=True)  34.4 us
    all_to_all x1, blocking collectives, on_device(): lax.all_to_all(outgoing, 'feat', split_axis=0, concat_axis=0, tiled=True)  28.7 us
    dot_general x1, matrix products, on_device(): lax.dot_general(turned.astype(jnp.bfloat16), rows, (((2,), (2,)), ((0,),...  26.1 us
    all_to_all x1, waiting for transfers between devices, on_device(): lax.all_to_all(partial_value, 'ex', split_axis=0, concat_axis=0, tiled=True)  25.7 us
    dot_general x1, matrix products, on_device(): jnp.einsum('ca,eab->ceb', table_a, signed.reshape(examples, HA, HB), pref...  13.9 us
    convert_element_type x1, other arithmetic, hadamard_rows(): return ((1 - 2 * parity).astype(jnp.float32) * scale).astype(jnp.bfloat16)  10.6 us
    unnamed x7, local copies, waits for them, and re-layouts  8.78 us
    mul x1, other arithmetic, on_device(): signed = grads * (1 - 2 * sign_bits).astype(jnp.bfloat16)[None, :]  8.52 us
  transfers between devices with their start and end apart: 1, of which 1 were waited for; matrix products, arithmetic and copies ran while one was open for 0% of the time, Pallas kernels for 0%

profile of v1, /device:TPU:8, one launch (start us, length us, event | category | flops | bytes accessed | tf_op | source)
XLA Modules:
  0.0 179.2 jit_solution(16965702583146081858)
XLA Ops:
  0.0 0.0 copy-start
  0.0 1.2 subtract_convert_fusion
  1.3 8.5 %broadcast_multiply_fusion = bf16[64,131072]{1,0:T(8,128)(2,1)S(1)} fusion(bf16[64,131072]{1,0:T(8,128)(2,1)} %param.5, bf16[131072]{0:T(1024)(128)(2,1)S(1)} %subtract_convert_fusion), kind=kLoop, calls=%fused_computation.15 | loop fusion | flops 8388608 | bytes 33816576 | tf_op jit(solution)/shard_map/mul | solution.py:53
  9.8 8.8 %copy.10 = bf16[8,8,256,512]{3,2,1,0:T(8,128)(2,1)} copy(bf16[8,8,256,512]{3,1,2,0:T(8,128)(2,1)S(1)} %bitcast.24) | data formatting | bytes 33554432
  18.6 0.0 copy-start.1
  18.6 13.9 %fusion.10 = bf16[256,64,512]{2,0,1:T(8,128)(2,1)} fusion(bf16[64,256,512]{2,1,0:T(8,128)(2,1)} %bitcast.23), kind=kOutput, calls=%fused_computation.24 | convolution fusion | flops 4296867840 | bytes 33554432 | tf_op jit(solution)/shard_map/ca,eab->ceb/dot_general | solution.py:55
  32.5 0.0 copy-done.1
  32.5 10.6 %fusion.6 = bf16[32,256,512]{2,1,0:T(8,128)(2,1)} fusion(s32[32,256]{1,0:T(8,128)S(1)} %and.95), kind=kLoop, calls=%fused_computation.13 | loop fusion | flops 71303168 | bytes 8421376 | tf_op jit(solution)/shard_map/convert_element_type | solution.py:28
  43.1 26.1 %fusion.5 = bf16[256,64,32]{1,2,0:T(8,128)(2,1)} fusion(bf16[256,64,512]{2,0,1:T(8,128)(2,1)} %fusion.10, bf16[32,256,512]{2,1,0:T(8,128)(2,1)} %fusion.6), kind=kOutput, calls=%fused_computation.12 | convolution fusion | flops 536870912 | bytes 26214400 | tf_op jit(solution)/shard_map/dot_general | solution.py:59
  69.3 0.0 copy-start.2
  69.3 2.8 %copy.8 = bf16[256,64,32]{0,1,2:T(8,128)(2,1)S(1)} copy(bf16[256,64,32]{1,2,0:T(8,128)(2,1)} %fusion.5) | data formatting | bytes 2097152 | tf_op jit(solution)/shard_map/dot_general | solution.py:59
  72.1 0.1 multiply_bitcast_fusion
  72.2 28.7 %all_to_all.20 = bf16[32,64,256]{2,1,0:T(8,128)(2,1)S(1)} all-to-all(bf16[32,64,256]{2,1,0:T(8,128)(2,1)S(1)} %multiply_bitcast_fusion), channel_id=1, replica_groups=mesh['feat'=32,'ex'=4] {'feat'}, dimensions={0} | all-to-all | bytes 2097152 | tf_op jit(solution)/shard_map/all_to_all | solution.py:69
  100.9 0.2 convert_reduce_fusion.1
  101.1 7.0 %all_to_all.21 = bf16[4,64,256]{2,1,0:T(8,128)(2,1)S(1)} all-to-all(bf16[4,64,256]{2,1,0:T(8,128)(2,1)S(1)} %stack.2), channel_id=1, replica_groups=mesh['feat'=32,'ex'=4] {'ex'}, dimensions={0} | all-to-all | bytes 262144 | tf_op jit(solution)/shard_map/all_to_all | solution.py:72
  108.1 0.0 copy-done
  108.1 2.1 %fusion.8 = bf16[4,8,64,512]{3,2,1,0:T(8,128)(2,1)} fusion(bf16[8,512,256,1]{2,1,0,3:T(8,128)(2,1)S(1)} %bitcast.22, bf16[4,64,256]{2,1,0:T(8,128)(2,1)S(1)} %all_to_all.21), kind=kOutput, calls=%fused_computation.19 | convolution fusion | flops 538968064 | bytes 4325376 | tf_op jit(solution)/shard_map/dot_general | solution.py:77
  110.1 4.4 %all-to-all-start.2 = ((bf16[4,8,64,512]{3,2,1,0:T(8,128)(2,1)}), bf16[4,8,64,512]{3,2,1,0:T(8,128)(2,1)}, u32[]{:S(2)}, u32[]{:S(2)}) async-start(bf16[4,8,64,512]{3,2,1,0:T(8,128)(2,1)} %fusion.8), calls=%async_computation.2 | async-start | bytes 4194304 | tf_op jit(solution)/shard_map/all_to_all | solution.py:85
  114.6 0.0 copy-done.2
  114.6 25.7 %all-to-all-done.2 = bf16[4,8,64,512]{3,2,1,0:T(8,128)(2,1)} async-done(((bf16[4,8,64,512]{3,2,1,0:T(8,128)(2,1)}), bf16[4,8,64,512]{3,2,1,0:T(8,128)(2,1)}, u32[]{:S(2)}, u32[]{:S(2)}) %all-to-all-start.2) | async-done | bytes 2097184 | tf_op jit(solution)/shard_map/all_to_all | solution.py:85
  140.3 3.6 %gather_fusion = bf16[32,64,512]{2,1,0:T(8,128)(2,1)} fusion(bf16[32,64,512]{2,1,0:T(8,128)(2,1)} %bitcast.8, s32[1024]{0:T(1024)S(1)} %pad_clamp_fusion), kind=kCustom, calls=%fused_computation | custom fusion | bytes 4194432 | tf_op jit(solution)/shard_map/jit(_take)/gather | solution.py:86
  143.9 34.4 %all_to_all.22 = bf16[32,64,512]{2,1,0:T(8,128)(2,1)S(1)} all-to-all(bf16[32,64,512]{2,1,0:T(8,128)(2,1)} %gather_fusion), channel_id=1, replica_groups=mesh['feat'=32,'ex'=4] {'feat'}, dimensions={0} | all-to-all | bytes 4194304 | tf_op jit(solution)/shard_map/all_to_all | solution.py:87
  178.3 0.9 convert_reduce_fusion
  (7 shorter events, 0.1 us)
Async XLA Ops:
  0.0 108.1 %copy-start = (bf16[4096,256]{1,0:T(8,128)(2,1)S(1)}, bf16[4096,256]{1,0:T(8,128)(2,1)}, u32[]{:S(2)}) copy-start(bf16[4096,256]{1,0:T(8,128)(2,1)} %param.8) | copy-start | bytes 6291460
  18.6 14.0 %copy-start.1 = (s32[8192]{0:T(1024)S(1)}, s32[8192]{0:T(1024)}, u32[]{:S(2)}) copy-start(s32[8192]{0:T(1024)} %param.7) | copy-start | bytes 98308
  69.3 45.3 %copy-start.2 = (s32[32]{0:T(128)S(1)}, s32[32]{0:T(128)}, u32[]{:S(2)}) copy-start(s32[32]{0:T(128)} %param.9) | copy-start | bytes 388
  110.1 30.2 %all-to-all-start.2 = ((bf16[4,8,64,512]{3,2,1,0:T(8,128)(2,1)}), bf16[4,8,64,512]{3,2,1,0:T(8,128)(2,1)}, u32[]{:S(2)}, u32[]{:S(2)}) async-start(bf16[4,8,64,512]{3,2,1,0:T(8,128)(2,1)} %fusion.8), calls=%async_computation.2 | async-start | bytes 4194304 | tf_op jit(solution)/shard_map/all_to_all | solution.py:85
